TPU v7x, 128 devices: a whole 4x4x4 slice. The times are simulated.
128 devices in a mesh: band: 4 (over z), sector: 32 (over y, x, core).
Axes of the slice: x: 4, y: 4, z: 4, core: 2. Of those that a mesh axis runs over, the one named last changes fastest.
Arguments:
- control: float32 [762, 64, 4096], P(None, 'band', 'sector'), may hold values from -16 to 16
- direction: float32 [762, 64, 4096], P(None, 'band', 'sector'), may hold values from -16 to 16
- step_lengths: float32 [4], replicated, may hold values from 0.25 to 2
- level_root: bfloat16 [762, 762], replicated, may hold values from -0.21875 to 0.21875
- lon_decay: float32 [762], replicated, as said below
- lat_decay: float32 [762], replicated, as said below
- obs_operator: bfloat16 [128, 762], replicated, may hold values from -0.21875 to 0.21875
- obs_values: float32 [131072, 128], P(('band', 'sector')), may hold values from -6 to 6
- obs_inv_err: float32 [131072, 128], P(('band', 'sector')), may hold values from 0.5 to 2
- obs_cols: int32 [131072], P(('band', 'sector')), may hold values from 0 to 1918, as said below
- obs_weights: float32 [131072, 4], P(('band', 'sector')), may hold values from 0.1 to 1
- counts: int32 [128, 128], P(('band', 'sector')), may hold values from 1 to 8, as said below
Outputs:
- departures: float32 [131072, 4, 128], P(('band', 'sector'))
- costs: float32 [4], replicated
Inputs may be any that keep to these rules, and one draw needn't show every extreme that they name: `lon_decay`: every line's coefficient lies strictly between 0 and 1. `lat_decay`: every line's coefficient lies strictly between 0 and 1. `obs_cols`: a column lat * 128 + lon of the owner's block with lat <= 14 and lon <= 126; unused slots hold such columns too. `counts`: in every draw some owner receives 8 rows from every device, and some device fills all its slots to every owner.
All inputs are finite; a program needn't handle non-finite values.
Results may differ from a plain program's by a relative error of at most 0.0039.
Values sent between devices are 32-bit elements; how exact they have to be, the bound alone decides.
No kernel may reach another device: no remote copies, remote signals or barrier semaphores. Data moves between devices by JAX's collectives and lax.ppermute only.
A program may use at most 256 MiB of HBM per device.

v0:
```python
import functools

import jax
import jax.numpy as jnp
from jax import lax
from jax.experimental import pallas as pl
from jax.experimental.pallas import tpu as pltpu
from jax.sharding import PartitionSpec as P

LANES = 128
LINE_TILE = 256


def padded_lines(n):
    return -(-n // LINE_TILE) * LINE_TILE


def local_filter_kernel(lat_dev, lon_dev, x_ref, mix_ref, a_ref, b_ref, out_ref, end_ref, work):
    chunks, rows, _ = out_ref.shape
    block = 256

    def mix_rows(c, carry):
        at = pl.ds(pl.multiple_of(c * block, block), block)
        res = jnp.dot(x_ref[at, :], mix_ref[...], preferred_element_type=jnp.float32)
        for lc in range(chunks):
            work[lc, at, :] = res[:, lc * LANES:(lc + 1) * LANES]
        return carry

    lax.fori_loop(0, rows // block, mix_rows, 0)

    def lon_step(j, states):
        at = pl.ds(pl.multiple_of(j * lat_dev, lat_dev), lat_dev)
        new = []
        for lc in range(chunks):
            state = a_ref[lc] * states[lc] + work[lc, at, :]
            work[lc, at, :] = state
            new.append(state)
        return tuple(new)

    zero = jnp.zeros((lat_dev, LANES), jnp.float32)
    ends = lax.fori_loop(0, lon_dev, lon_step, (zero,) * chunks)
    for lc in range(chunks):
        end_ref[lc] = ends[lc]

    for lc in range(chunks):
        first = work[lc, pl.ds(0, lon_dev, stride=lat_dev), :]
        out_ref[lc, pl.ds(0, lon_dev), :] = first

        def lat_step(i, state, lc=lc):
            state = b_ref[lc] * state + work[lc, pl.ds(i, lon_dev, stride=lat_dev), :]
            out_ref[lc, pl.ds(pl.multiple_of(i * lon_dev, lon_dev), lon_dev), :] = state
            return state

        lax.fori_loop(1, lat_dev, lat_step, first)


def local_filter(xt, mix, a_rows, b_rows, lat_dev, lon_dev):
    trials, positions, klen = xt.shape
    kpad = mix.shape[1]
    chunks = kpad // LANES
    flops = 2 * positions * klen * kpad * trials + 4 * trials * positions * kpad
    bytes_accessed = xt.size * 2 + trials * positions * kpad * 4 + mix.size * 2
    return pl.pallas_call(
        functools.partial(local_filter_kernel, lat_dev, lon_dev),
        grid=(trials,),
        in_specs=[
            pl.BlockSpec((None, positions, klen), lambda t: (t, 0, 0)),
            pl.BlockSpec((klen, kpad), lambda t: (0, 0)),
            pl.BlockSpec((chunks, lat_dev, LANES), lambda t: (0, 0, 0)),
            pl.BlockSpec((chunks, lon_dev, LANES), lambda t: (0, 0, 0)),
        ],
        out_specs=[
            pl.BlockSpec((None, chunks, positions, LANES), lambda t: (t, 0, 0, 0)),
            pl.BlockSpec((None, chunks, lat_dev, LANES), lambda t: (t, 0, 0, 0)),
        ],
        out_shape=[
            jax.ShapeDtypeStruct((trials, chunks, positions, LANES), jnp.float32),
            jax.ShapeDtypeStruct((trials, chunks, lat_dev, LANES), jnp.float32),
        ],
        scratch_shapes=[pltpu.VMEM((chunks, positions, LANES), jnp.float32)],
        compiler_params=pltpu.CompilerParams(
            dimension_semantics=("arbitrary",), vmem_limit_bytes=48 * 1024 * 1024
        ),
        cost_estimate=pl.CostEstimate(
            flops=flops, bytes_accessed=bytes_accessed, transcendentals=0
        ),
    )(xt, mix, a_rows, b_rows)


def shifted(x, axis, shift):
    n = lax.axis_size(axis)
    return lax.ppermute(x, axis, [(s, (s + shift) % n) for s in range(n)])


def xor_total(x, axes):
    for axis in axes:
        n = lax.axis_size(axis)
        bit = 1
        while bit < n:
            x = x + lax.ppermute(x, axis, [(s, s ^ bit) for s in range(n)])
            bit *= 2
    return x


def body(
    control,
    direction,
    step_lengths,
    level_root,
    lon_decay,
    lat_decay,
    obs_operator,
    obs_values,
    obs_inv_err,
    obs_cols,
    obs_weights,
    counts,
):
    num_lines, lat_dev, lon_dev = control.shape
    trials = step_lengths.shape[0]
    channels = obs_values.shape[1]
    bands = lax.axis_size("band")
    sectors = lax.axis_size("sector")
    devices_all = bands * sectors
    capacity = obs_cols.shape[0] // devices_all
    kpad = padded_lines(num_lines)
    extra = kpad - num_lines
    f32 = jnp.float32

    packed = jnp.concatenate(
        [obs_cols.astype(f32)[:, None], obs_weights], axis=1
    ).reshape(devices_all, capacity, 5)
    packed = lax.all_gather(packed, ("band", "sector"))
    packed = lax.dynamic_index_in_dim(packed, lax.axis_index(("band", "sector")), 1, False)

    trial_fields = control[None] + step_lengths[:, None, None, None] * direction[None]
    background = jnp.sum(trial_fields * trial_fields, axis=(1, 2, 3))
    xt = jnp.transpose(trial_fields.astype(jnp.bfloat16), (0, 3, 2, 1))
    xt = jnp.pad(xt.reshape(trials, lon_dev * lat_dev, num_lines), ((0, 0), (0, 0), (0, extra)))
    mix_t = jnp.pad(level_root, ((0, extra), (0, extra))).T

    a = jnp.pad(lon_decay, (0, extra), constant_values=0.5)
    b = jnp.pad(lat_decay, (0, extra), constant_values=0.5)
    chunks = kpad // LANES

    def by_chunk(v):
        v = v.reshape(v.shape[:-1] + (chunks, LANES))
        return jnp.moveaxis(v, -2, 0)

    a_c = by_chunk(a)
    b_c = by_chunk(b)
    log_a_c = jnp.log(a_c)
    log_b_c = jnp.log(b_c)
    a_rows = jnp.broadcast_to(a_c[:, None, :], (chunks, lat_dev, LANES))
    b_rows = jnp.broadcast_to(b_c[:, None, :], (chunks, lon_dev, LANES))

    local, lon_ends = local_filter(xt, mix_t, a_rows, b_rows, lat_dev, lon_dev)
    local = local.reshape(trials, chunks, lat_dev, lon_dev, LANES)

    per_line = lambda v: v[None, :, None, :]
    carried = shifted(lon_ends, "sector", 1)
    carried = carried + per_line(jnp.exp(log_a_c * lon_dev)) * shifted(lon_ends, "sector", 2)
    span = 2
    while span < sectors:
        gain = jnp.exp(log_a_c * (lon_dev * span))
        carried = carried + per_line(gain) * shifted(carried, "sector", span)
        span *= 2
    loop_gain = 1.0 - jnp.exp(log_a_c * (lon_dev * sectors))
    incoming = carried / per_line(loop_gain)

    rows = []
    state = jnp.zeros((trials, chunks, LANES), f32)
    for i in range(lat_dev):
        state = b_c[None] * state + incoming[:, :, i, :]
        rows.append(state)
    incoming_lat = jnp.stack(rows, axis=2)
    lon_rise = jnp.exp(log_a_c[:, None, :] * jnp.arange(1, lon_dev + 1).astype(f32)[None, :, None])
    lat_rise = jnp.exp(log_b_c[:, None, :] * jnp.arange(1, lat_dev + 1).astype(f32)[None, :, None])
    scale_a = jnp.sqrt(1.0 - a_c * a_c)[:, None, :]
    scale_b = jnp.sqrt(1.0 - b_c * b_c)[:, None, None, :]

    band_end = scale_a * (
        local[:, :, lat_dev - 1] + lon_rise[None] * incoming_lat[:, :, lat_dev - 1, None, :]
    )
    band_ends = lax.all_gather(band_end, "band")
    me = lax.axis_index("band")
    source = jnp.arange(bands)
    power = (me - 1 - source).astype(f32)
    band_weight = jnp.where(
        (source < me)[:, None, None],
        jnp.exp(log_b_c[None] * (lat_dev * power)[:, None, None]),
        0.0,
    )
    entering = jnp.sum(band_weight[:, None, :, None, :] * band_ends, axis=0)

    increment = scale_b * (
        scale_a[:, None] * (local + lon_rise[None, :, None] * incoming_lat[:, :, :, None, :])
        + lat_rise[None, :, :, None, :] * entering[:, :, None, :, :]
    )
    increment = jnp.moveaxis(increment.reshape(trials, chunks, lat_dev * lon_dev, LANES), 1, 2)
    increment = increment.reshape(trials, lat_dev * lon_dev, kpad)

    where = packed[:, :, 0].astype(jnp.int32).reshape(-1, 1)
    weights = packed[:, :, 1:].reshape(-1, 4)
    position = jnp.arange(lat_dev * lon_dev, dtype=jnp.int32)[None, :]
    interp = None
    for corner, offset in enumerate((0, 1, lon_dev, lon_dev + 1)):
        term = jnp.where(position == where + offset, weights[:, corner, None], 0.0)
        interp = term if interp is None else interp + term
    profile = jnp.einsum(
        "rp,tpn->trn", interp, increment, precision=lax.Precision.HIGH,
        preferred_element_type=f32,
    ).astype(jnp.bfloat16)
    operator = jnp.pad(obs_operator, ((0, 0), (0, extra)))
    evolved = jnp.einsum(
        "trn,on->rto", profile, operator, preferred_element_type=f32
    ).reshape(devices_all, capacity, trials, channels)
    returned = lax.all_to_all(evolved, ("band", "sector"), 0, 0, tiled=True)

    observed = obs_values.reshape(devices_all, capacity, 1, channels)
    inverse = obs_inv_err.reshape(devices_all, capacity, 1, channels)
    live = counts[0][:, None] > jnp.arange(capacity, dtype=jnp.int32)[None, :]
    weighted = (returned - observed) * inverse
    departures = jnp.where(live[:, :, None, None], weighted, 0.0)
    misfit = jnp.sum(departures * departures, axis=(0, 1, 3))

    totals = xor_total(jnp.stack([background, misfit]), ("sector", "band"))
    cell_count = num_lines * lat_dev * lon_dev * devices_all
    cost_values = 0.5 * (totals[0] + totals[1]) / cell_count
    return (departures.reshape(devices_all * capacity, trials, channels), cost_values)


def solution(mesh):
    placed = (
        P(None, "band", "sector"),
        P(None, "band", "sector"),
        P(),
        P(),
        P(),
        P(),
        P(),
        P(("band", "sector"), None),
        P(("band", "sector"), None),
        P(("band", "sector")),
        P(("band", "sector"), None),
        P(("band", "sector"), None),
    )
    return jax.shard_map(
        body,
        mesh=mesh,
        in_specs=placed,
        out_specs=(P(("band", "sector"), None, None), P()),
        check_vma=False,
    )
```

profile of v0, /device:TPU:0, one launch (start us, length us, event | category | flops | bytes accessed | tf_op | source)
XLA Modules:
  0.0 367.0 jit_solution(4238253751395974622)
XLA Ops:
  7.2 0.9 concatenate.9
  8.2 0.7 convert_element_type.67
  9.0 0.6 pad_maximum_fusion
  9.7 6.7 %copy.78 = f32[762,16,128]{0,1,2:T(8,128)} copy(f32[762,16,128]{2,1,0:T(8,128)} %param.12) | data formatting | bytes 12484608 | tf_op args[0]
  16.4 6.8 %copy.79 = f32[762,16,128]{0,1,2:T(8,128)} copy(f32[762,16,128]{2,1,0:T(8,128)} %param.13) | data formatting | bytes 12484608 | tf_op args[1]
  23.2 0.6 copy.80
  23.9 7.2 %add_convert_fusion = bf16[4,2048,762]{2,1,0:T(8,128)(2,1)S(1)} fusion(f32[2048,762]{1,0:T(8,128)} %bitcast.110, f32[4]{0:T(128)S(1)} %copy-done.6, f32[2048,762]{1,0:T(8,128)} %bitcast.109), kind=kLoop, calls=%fused_computation.6 | loop fusion | flops 18726912 | bytes 24969232 | tf_op jit(solution)/shard_map/convert_element_type | solution.py:138
  31.1 6.5 %pad.22.x_ref = bf16[4,2048,768]{2,1,0:T(8,128)(2,1)} pad(bf16[4,2048,762]{2,1,0:T(8,128)(2,1)S(1)} %add_convert_fusion, bf16[]{:T(256)} %constant.21.clone.1), padding=0_0x0_0x0_6 | pad | bytes 25067522 | tf_op jit(solution)/shard_map/jit(_pad)/pad | solution.py:139
  37.8 39.6 %shard_map.131 = (f32[4,6,2048,128]{3,2,1,0:T(8,128)}, f32[4,6,16,128]{3,2,1,0:T(8,128)S(1)}) custom-call(bf16[4,2048,768]{2,1,0:T(8,128)(2,1)} %pad.22.x_ref, bf16[768,768]{1,0:T(8,128)(2,1)S(1)} %pad_bitcast_fusion.mix_ref, f32[6,16,128]{2,1,0:T(8,128)S(1)} %broadcast_in_dim.102.a_ref, f32[6,128,128]{2,1,0:T(8,128)S(1)} %broadcast_in_dim.103.b_ref), custom_call_target="tpu_custom_call" | custom-call | flops 9688842240 | bytes 38928384 | tf_op jit(solution)/shard_map/pallas_call | solution.py:63
  77.4 1.6 collective-permute-start.1
  79.0 8.3 %collective-permute-done = f32[4,6,16,128]{3,2,1,0:T(8,128)S(1)} collective-permute-done((f32[4,6,16,128]{3,2,1,0:T(8,128)S(1)}, f32[4,6,16,128]{3,2,1,0:T(8,128)S(1)}, u32[]{:S(2)}, u32[]{:S(2)}) %collective-permute-start) | collective-permute-done | bytes 196640 | tf_op jit(solution)/shard_map/ppermute | solution.py:92
  87.3 1.2 collective-permute-done.1
  88.6 10.7 %collective-permute-done.2 = f32[4,6,16,128]{3,2,1,0:T(8,128)S(1)} collective-permute-done((f32[4,6,16,128]{3,2,1,0:T(8,128)S(1)}, f32[4,6,16,128]{3,2,1,0:T(8,128)S(1)}, u32[]{:S(2)}, u32[]{:S(2)}) %collective-permute-start.2) | collective-permute-done | bytes 196640 | tf_op jit(solution)/shard_map/ppermute | solution.py:92
  99.4 10.6 %collective-permute-done.3 = f32[4,6,16,128]{3,2,1,0:T(8,128)S(1)} collective-permute-done((f32[4,6,16,128]{3,2,1,0:T(8,128)S(1)}, f32[4,6,16,128]{3,2,1,0:T(8,128)S(1)}, u32[]{:S(2)}, u32[]{:S(2)}) %collective-permute-start.3) | collective-permute-done | bytes 196640 | tf_op jit(solution)/shard_map/ppermute | solution.py:92
  110.2 7.3 %collective-permute-done.4 = f32[4,6,16,128]{3,2,1,0:T(8,128)S(1)} collective-permute-done((f32[4,6,16,128]{3,2,1,0:T(8,128)S(1)}, f32[4,6,16,128]{3,2,1,0:T(8,128)S(1)}, u32[]{:S(2)}, u32[]{:S(2)}) %collective-permute-start.4) | collective-permute-done | bytes 196640 | tf_op jit(solution)/shard_map/ppermute | solution.py:92
  117.5 0.3 collective-permute-start.5
  117.9 7.0 %collective-permute-done.5 = f32[4,6,16,128]{3,2,1,0:T(8,128)S(1)} collective-permute-done((f32[4,6,16,128]{3,2,1,0:T(8,128)S(1)}, f32[4,6,16,128]{3,2,1,0:T(8,128)S(1)}, u32[]{:S(2)}, u32[]{:S(2)}) %collective-permute-start.5) | collective-permute-done | bytes 196640 | tf_op jit(solution)/shard_map/ppermute | solution.py:92
  125.2 2.8 fusion.32
  128.3 0.3 stack.8
  128.6 2.5 constant_dynamic-slice_fusion
  131.1 0.8 copy.97
  132.5 6.5 %fusion.46 = f32[1024,2048,1]{1,0,2:T(8,128)} fusion(f32[1024]{0:T(1024)S(1)} %bitcast.118, s32[1024]{0:T(1024)S(1)} %get-tuple-element.37, f32[1024]{0:T(1024)S(1)} %bitcast.119, s32[1024]{0:T(1024)S(1)} %get-tuple-element.38, f32[1024]{0:T(1024)S(1)} %bitcast.120, s32[1024]{0:T(1024)S(1)} %get-tuple-element.36, f32[1024]{0:T(1024)S(1)} %bitcast.117, ...), kind=kLoop, calls=%fused_computation.9.clone.1 | loop fusion | flops 23068672 | bytes 8421376 | tf_op jit(solution)/shard_map/rp,tpn->trn/dot_general | solution.py:210
  139.0 52.5 %all-gather.3.cloned.1.call-done = f32[4,4,6,128,128]{4,3,2,1,0:T(8,128)} async-done(((f32[1,4,6,128,128]{4,3,2,1,0:T(8,128)}), f32[4,4,6,128,128]{4,3,2,1,0:T(8,128)}) %all-gather.3.cloned.1.call-update) | async-done | bytes 6291472 | tf_op jit(solution)/shard_map/all_gather | solution.py:185
  191.5 3.8 %multiply_reduce_fusion.1 = f32[4,6,128,128]{3,2,1,0:T(8,128)S(1)} fusion(f32[4,4,6,128,128]{4,3,2,1,0:T(8,128)} %all-gather.3.cloned.1.call-done, f32[4,6,128]{2,1,0:T(8,128)S(1)} %exponential_select_fusion), kind=kLoop, calls=%fused_computation.24 | loop fusion | flops 2752512 | bytes 7876608 | tf_op jit(solution)/shard_map/reduce_sum | solution.py:194
  195.3 0.8 mul.561
  196.0 0.4 mul.611
  196.5 18.4 %fusion.1 = f32[4,6,2048,128]{3,2,1,0:T(8,128)} fusion(f32[4,6,2048,128]{3,2,1,0:T(8,128)} %get-tuple-element.4, f32[4,6,128,128]{3,2,1,0:T(8,128)S(1)} %multiply_reduce_fusion.1, f32[6,2048,128]{2,1,0:T(8,128)S(1)} %bitcast.108, f32[4,6,16,128]{3,2,1,0:T(8,128)S(1)} %stack.8, f32[6,2048,128]{2,1,0:T(8,128)S(1)} %bitcast.107, ...), kind=kLoop, calls=%fused_computation.2 | loop fusion | flops 37748736 | bytes 64690176 | tf_op jit(solution)/shard_map/mul | solution.py:196
  214.9 24.8 %copy.84 = f32[4,2048,6,128]{1,3,2,0:T(8,128)} copy(f32[4,2048,6,128]{3,1,2,0:T(8,128)} %bitcast.104) | data formatting | bytes 50331648 | tf_op jit(solution)/shard_map/transpose | solution.py:200
  239.6 45.1 %fusion.4 = bf16[4,768,1024]{2,1,0:T(8,128)(2,1)S(1)} fusion(f32[4,2048,768]{1,2,0:T(8,128)} %bitcast.106, f32[1024,2048,1]{1,0,2:T(8,128)} %fusion.46), kind=kOutput, calls=%fused_computation.8 | convolution fusion | flops 38654705664 | bytes 39845888 | tf_op jit(solution)/shard_map/rp,tpn->trn/dot_general | solution.py:210
  284.8 2.3 fusion.27
  287.1 1.9 copy.91
  289.0 1.6 copy.92
  290.7 9.2 %all-to-all-start = ((f32[128,8,4,128]{3,1,2,0:T(8,128)}), f32[128,8,4,128]{3,1,2,0:T(8,128)S(1)}, u32[]{:S(2)}, u32[]{:S(2)}) async-start(f32[128,8,4,128]{3,1,2,0:T(8,128)} %copy.92), calls=%async_computation | async-start | bytes 4194304 | tf_op jit(solution)/shard_map/all_to_all | solution.py:218
  300.0 9.0 %multiply_reduce_fusion = f32[4]{0:T(128)S(1)} fusion(f32[762,16,128]{2,1,0:T(8,128)} %param.13, f32[4]{0:T(128)S(1)} %copy-done.6, f32[762,16,128]{2,1,0:T(8,128)} %param.12), kind=kLoop, calls=%fused_computation.7 | loop fusion | flops 24969212 | bytes 12484640 | tf_op jit(solution)/shard_map/reduce_sum | solution.py:137
  309.0 21.2 %all-to-all-done = f32[128,8,4,128]{3,1,2,0:T(8,128)S(1)} async-done(((f32[128,8,4,128]{3,1,2,0:T(8,128)}), f32[128,8,4,128]{3,1,2,0:T(8,128)S(1)}, u32[]{:S(2)}, u32[]{:S(2)}) %all-to-all-start) | async-done | bytes 2097184 | tf_op jit(solution)/shard_map/all_to_all | solution.py:218
  330.2 0.5 multiply_reduce_fusion.2
  330.8 2.7 copy.94
  333.5 0.7 collective-permute-start.7
  334.2 3.0 collective-permute-done.7
  337.2 0.7 collective-permute-start.8
  337.8 4.5 %collective-permute-done.8 = f32[2,4]{1,0:T(2,128)S(1)} collective-permute-done((f32[2,4]{1,0:T(2,128)S(1)}, f32[2,4]{1,0:T(2,128)S(1)}, u32[]{:S(2)}, u32[]{:S(2)}) %collective-permute-start.8) | collective-permute-done | bytes 64 | tf_op jit(solution)/shard_map/ppermute | solution.py:100
  342.5 3.4 collective-permute-done.9
  346.2 4.8 %collective-permute-done.10 = f32[2,4]{1,0:T(2,128)S(1)} collective-permute-done((f32[2,4]{1,0:T(2,128)S(1)}, f32[2,4]{1,0:T(2,128)S(1)}, u32[]{:S(2)}, u32[]{:S(2)}) %collective-permute-start.10) | collective-permute-done | bytes 64 | tf_op jit(solution)/shard_map/ppermute | solution.py:100
  351.0 0.4 collective-permute-start.11
  351.4 3.2 collective-permute-done.11
  354.6 0.4 collective-permute-start.12
  355.0 4.7 %collective-permute-done.12 = f32[2,4]{1,0:T(2,128)S(1)} collective-permute-done((f32[2,4]{1,0:T(2,128)S(1)}, f32[2,4]{1,0:T(2,128)S(1)}, u32[]{:S(2)}, u32[]{:S(2)}) %collective-permute-start.12) | collective-permute-done | bytes 64 | tf_op jit(solution)/shard_map/ppermute | solution.py:100
  359.7 0.5 multiply_bitcast_fusion
  (71 shorter events, 2.7 us)
Async XLA Ops:
  7.2 121.4 %all-gather.5.cloned.1.call-start = ((), (), s32[]{:S(2)}) async-start(), calls=%async_computation.2 | async-start | bytes 2641920 | tf_op jit(solution)/shard_map/all_gather | solution.py:133
  9.7 181.8 %all-gather.3.cloned.1.call-start = ((), (), s32[]{:S(2)}) async-start(), calls=%async_computation.1 | async-start | bytes 7864320 | tf_op jit(solution)/shard_map/all_gather | solution.py:185
  16.4 6.8 %copy-start = (bf16[762,762]{1,0:T(8,128)(2,1)S(1)}, bf16[762,762]{1,0:T(8,128)(2,1)}, u32[]{:S(2)}) copy-start(bf16[762,762]{1,0:T(8,128)(2,1)} %param.15) | copy-start | bytes 3483868
  16.4 7.5 %copy-start.6 = (f32[4]{0:T(128)S(1)}, f32[4]{0:T(128)}, u32[]{:S(2)}) copy-start(f32[4]{0:T(128)} %param.14) | copy-start | bytes 52
  31.1 6.6 %copy-start.5 = (f32[762]{0:T(1024)S(1)}, f32[762]{0:T(1024)}, u32[]{:S(2)}) copy-start(f32[762]{0:T(1024)} %param.17) | copy-start | bytes 9148
  31.1 6.6 %copy-start.4 = (f32[762]{0:T(1024)S(1)}, f32[762]{0:T(1024)}, u32[]{:S(2)}) copy-start(f32[762]{0:T(1024)} %param.16) | copy-start | bytes 9148
  77.4 9.9 %collective-permute-start = (f32[4,6,16,128]{3,2,1,0:T(8,128)S(1)}, f32[4,6,16,128]{3,2,1,0:T(8,128)S(1)}, u32[]{:S(2)}, u32[]{:S(2)}) collective-permute-start(f32[4,6,16,128]{3,2,1,0:T(8,128)S(1)} %get-tuple-element.5), channel_id=1, source_target_pairs={{0,1},{1,2},{2,3},{3,4},{4,5},{5,6},{6,7},{7,8},{8,9},{9,10},{10,1... | collective-permute-start | bytes 589832 | tf_op jit(solution)/shard_map/ppermute | solution.py:92
  77.4 11.1 %collective-permute-start.1 = (f32[4,6,16,128]{3,2,1,0:T(8,128)S(1)}, f32[4,6,16,128]{3,2,1,0:T(8,128)S(1)}, u32[]{:S(2)}, u32[]{:S(2)}) collective-permute-start(f32[4,6,16,128]{3,2,1,0:T(8,128)S(1)} %get-tuple-element.5), channel_id=1, source_target_pairs={{0,2},{1,3},{2,4},{3,5},{4,6},{5,7},{6,8},{7,9},{8,10},{9,11},{10,... | collective-permute-start | bytes 589832 | tf_op jit(solution)/shard_map/ppermute | solution.py:92
  88.5 10.8 %collective-permute-start.2 = (f32[4,6,16,128]{3,2,1,0:T(8,128)S(1)}, f32[4,6,16,128]{3,2,1,0:T(8,128)S(1)}, u32[]{:S(2)}, u32[]{:S(2)}) collective-permute-start(f32[4,6,16,128]{3,2,1,0:T(8,128)S(1)} %multiply_add_fusion.3), channel_id=1, source_target_pairs={{0,2},{1,3},{2,4},{3,5},{4,6},{5,7},{6,8},{7,9},{8,10},{9,11},{10,... | collective-permute-start | bytes 589832 | tf_op jit(solution)/shard_map/ppermute | solution.py:92
  99.3 10.7 %collective-permute-start.3 = (f32[4,6,16,128]{3,2,1,0:T(8,128)S(1)}, f32[4,6,16,128]{3,2,1,0:T(8,128)S(1)}, u32[]{:S(2)}, u32[]{:S(2)}) collective-permute-start(f32[4,6,16,128]{3,2,1,0:T(8,128)S(1)} %multiply_add_fusion.2), channel_id=1, source_target_pairs={{0,4},{1,5},{2,6},{3,7},{4,8},{5,9},{6,10},{7,11},{8,12},{9,13},{1... | collective-permute-start | bytes 589832 | tf_op jit(solution)/shard_map/ppermute | solution.py:92
  110.1 7.4 %collective-permute-start.4 = (f32[4,6,16,128]{3,2,1,0:T(8,128)S(1)}, f32[4,6,16,128]{3,2,1,0:T(8,128)S(1)}, u32[]{:S(2)}, u32[]{:S(2)}) collective-permute-start(f32[4,6,16,128]{3,2,1,0:T(8,128)S(1)} %multiply_add_fusion.1), channel_id=1, source_target_pairs={{0,8},{1,9},{2,10},{3,11},{4,12},{5,13},{6,14},{7,15},{8,16},{9,17... | collective-permute-start | bytes 589832 | tf_op jit(solution)/shard_map/ppermute | solution.py:92
  117.5 7.4 %collective-permute-start.5 = (f32[4,6,16,128]{3,2,1,0:T(8,128)S(1)}, f32[4,6,16,128]{3,2,1,0:T(8,128)S(1)}, u32[]{:S(2)}, u32[]{:S(2)}) collective-permute-start(f32[4,6,16,128]{3,2,1,0:T(8,128)S(1)} %multiply_add_fusion), channel_id=1, source_target_pairs={{0,16},{1,17},{2,18},{3,19},{4,20},{5,21},{6,22},{7,23},{8,24},{9,... | collective-permute-start | bytes 589832 | tf_op jit(solution)/shard_map/ppermute | solution.py:92
  239.6 45.2 %copy-start.3 = (bf16[128,762]{1,0:T(8,128)(2,1)S(1)}, bf16[128,762]{1,0:T(8,128)(2,1)}, u32[]{:S(2)}) copy-start(bf16[128,762]{1,0:T(8,128)(2,1)} %param.18) | copy-start | bytes 585220
  287.1 12.7 %copy-start.7 = (s32[1,128]{1,0:T(1,128)S(1)}, s32[1,128]{1,0:T(1,128)}, u32[]{:S(2)}) copy-start(s32[1,128]{1,0:T(1,128)} %param.23) | copy-start | bytes 1540
  290.7 39.5 %all-to-all-start = ((f32[128,8,4,128]{3,1,2,0:T(8,128)}), f32[128,8,4,128]{3,1,2,0:T(8,128)S(1)}, u32[]{:S(2)}, u32[]{:S(2)}) async-start(f32[128,8,4,128]{3,1,2,0:T(8,128)} %copy.92), calls=%async_computation | async-start | bytes 4194304 | tf_op jit(solution)/shard_map/all_to_all | solution.py:218
  299.8 30.4 %copy-start.1 = (f32[1024,128]{1,0:T(8,128)S(1)}, f32[1024,128]{1,0:T(8,128)}, u32[]{:S(2)}) copy-start(f32[1024,128]{1,0:T(8,128)} %param.20) | copy-start | bytes 1572868
  299.8 30.4 %copy-start.2 = (f32[1024,128]{1,0:T(8,128)S(1)}, f32[1024,128]{1,0:T(8,128)}, u32[]{:S(2)}) copy-start(f32[1024,128]{1,0:T(8,128)} %param.19) | copy-start | bytes 1572868
  330.7 2.8 collective-permute-start.6
  333.5 3.7 collective-permute-start.7
  337.2 5.2 %collective-permute-start.8 = (f32[2,4]{1,0:T(2,128)S(1)}, f32[2,4]{1,0:T(2,128)S(1)}, u32[]{:S(2)}, u32[]{:S(2)}) collective-permute-start(f32[2,4]{1,0:T(2,128)S(1)} %fusion.42), channel_id=1, source_target_pairs={{0,4},{1,5},{2,6},{3,7},{4,0},{5,1},{6,2},{7,3},{8,12},{9,13},{10,... | collective-permute-start | bytes 104 | tf_op jit(solution)/shard_map/ppermute | solution.py:100
  342.3 3.6 collective-permute-start.9
  345.9 5.1 %collective-permute-start.10 = (f32[2,4]{1,0:T(2,128)S(1)}, f32[2,4]{1,0:T(2,128)S(1)}, u32[]{:S(2)}, u32[]{:S(2)}) collective-permute-start(f32[2,4]{1,0:T(2,128)S(1)} %add.384), channel_id=1, source_target_pairs={{0,16},{1,17},{2,18},{3,19},{4,20},{5,21},{6,22},{7,23},{8,24},{9,... | collective-permute-start | bytes 104 | tf_op jit(solution)/shard_map/ppermute | solution.py:100
  351.0 3.6 collective-permute-start.11
  354.6 5.1 %collective-permute-start.12 = (f32[2,4]{1,0:T(2,128)S(1)}, f32[2,4]{1,0:T(2,128)S(1)}, u32[]{:S(2)}, u32[]{:S(2)}) collective-permute-start(f32[2,4]{1,0:T(2,128)S(1)} %add.386), channel_id=1, source_target_pairs={{0,64},{32,96},{64,0},{96,32},{1,65},{33,97},{65,1},{97,33},{2,66}... | collective-permute-start | bytes 104 | tf_op jit(solution)/shard_map/ppermute | solution.py:100
Sparse Core Ops, SparseCore 0:
  11.1 68.1 all-gather.4
  128.2 63.2 all-gather.2
where the time goes:
time: 368 us; the launch traced here: 367 us
  waiting for transfers between devices  142 us (39%)
  local copies, waits for them, and re-layouts  58.3 us (16%)
  other arithmetic  50.9 us (14%)
  matrix products  47.5 us (13%)
  Pallas kernels  39.6 us (11%)
  between operations  14.4 us (4%)
  starting transfers between devices  14 us (4%)
    all_gather x1, waiting for transfers between devices, body(): band_ends = lax.all_gather(band_end, 'band')  52.5 us
    dot_general x1, matrix products, body(): jnp.einsum('rp,tpn->trn', interp, increment, precision=lax.Precision.HIGH...  45.1 us
    ppermute x6, waiting for transfers between devices, shifted(): return lax.ppermute(x, axis, [(s, (s + shift) % n) for s in range(n)])  45.1 us
    pallas_call x1, Pallas kernels, local_filter(): pl.pallas_call(functools.partial(local_filter_kernel, lat_dev, lon_dev),...  39.6 us
    transpose x1, local copies, waits for them, and re-layouts, body(): jnp.moveaxis(increment.reshape(trials, chunks, lat_dev * lon_dev, LANES),...  24.8 us
    ppermute x7, waiting for transfers between devices, xor_total(): x = x + lax.ppermute(x, axis, [(s, s ^ bit) for s in range(n)])  23.6 us
    all_to_all x1, waiting for transfers between devices, body(): returned = lax.all_to_all(evolved, ('band', 'sector'), 0, 0, tiled=True)  21.2 us
    mul x1, other arithmetic, body(): scale_b * (scale_a[:, None] * (local + lon_rise[None, :, None] * incoming...  18.4 us
  transfers between devices with their start and end apart: 16, of which 14 were waited for; matrix products, arithmetic and copies ran while one was open for 15% of the time, Pallas kernels for 11%

commit v1 on v0

--- a/solution.py
+++ b/solution.py
@@ -136,8 +136,8 @@
     trial_fields = control[None] + step_lengths[:, None, None, None] * direction[None]
     background = jnp.sum(trial_fields * trial_fields, axis=(1, 2, 3))
     xt = jnp.transpose(trial_fields.astype(jnp.bfloat16), (0, 3, 2, 1))
-    xt = jnp.pad(xt.reshape(trials, lon_dev * lat_dev, num_lines), ((0, 0), (0, 0), (0, extra)))
-    mix_t = jnp.pad(level_root, ((0, extra), (0, extra))).T
+    xt = xt.reshape(trials, lon_dev * lat_dev, num_lines)
+    mix_t = jnp.pad(level_root, ((0, extra), (0, 0))).T
 
     a = jnp.pad(lon_decay, (0, extra), constant_values=0.5)
     b = jnp.pad(lat_decay, (0, extra), constant_values=0.5)

time: 368 us -> 366 us (level)
  local copies, waits for them, and re-layouts: 58.3 us -> 51.7 us
  other arithmetic: 50.9 us -> 55.1 us
    pad x1 -> x0, local copies, waits for them, and re-layouts: 6.55 us -> none  [body(): jnp.pad(xt.reshape(trials, lon_dev * lat_dev, num_lines), ((0, 0), (0, 0)...]
    convert_element_type x1, other arithmetic: 7.17 us -> 11.4 us  [body(): xt = jnp.transpose(trial_fields.astype(jnp.bfloat16), (0, 3, 2, 1))]
  transfers between devices with their start and end apart: 16 -> 16, of which waited for: 14 -> 14; matrix products, arithmetic and copies ran while one was open for 15% -> 14% of each run, Pallas kernels for 11% -> 11%
where the time goes in v1:
time: 366 us; the launch traced here: 365 us
  waiting for transfers between devices  142 us (39%)
  other arithmetic  55.1 us (15%)
  local copies, waits for them, and re-layouts  51.7 us (14%)
  matrix products  47.5 us (13%)
  Pallas kernels  39.6 us (11%)
  between operations  14.4 us (4%)
  starting transfers between devices  14 us (4%)
    all_gather x1, waiting for transfers between devices, body(): band_ends = lax.all_gather(band_end, 'band')  52.5 us
    dot_general x1, matrix products, body(): jnp.einsum('rp,tpn->trn', interp, increment, precision=lax.Precision.HIGH...  45.1 us
    ppermute x6, waiting for transfers between devices, shifted(): return lax.ppermute(x, axis, [(s, (s + shift) % n) for s in range(n)])  45.1 us
    pallas_call x1, Pallas kernels, local_filter(): pl.pallas_call(functools.partial(local_filter_kernel, lat_dev, lon_dev),...  39.6 us
    transpose x1, local copies, waits for them, and re-layouts, body(): jnp.moveaxis(increment.reshape(trials, chunks, lat_dev * lon_dev, LANES),...  24.8 us
    ppermute x7, waiting for transfers between devices, xor_total(): x = x + lax.ppermute(x, axis, [(s, s ^ bit) for s in range(n)])  23.6 us
    all_to_all x1, waiting for transfers between devices, body(): returned = lax.all_to_all(evolved, ('band', 'sector'), 0, 0, tiled=True)  21.2 us
    mul x1, other arithmetic, body(): scale_b * (scale_a[:, None] * (local + lon_rise[None, :, None] * incoming...  18.4 us
  transfers between devices with their start and end apart: 16, of which 14 were waited for; matrix products, arithmetic and copies ran while one was open for 14% of the time, Pallas kernels for 11%

profile of v1, /device:TPU:0, one launch (start us, length us, event | category | flops | bytes accessed | tf_op | source)
XLA Modules:
  0.0 364.7 jit_solution(515866553921433058)
XLA Ops:
  7.2 0.9 concatenate.9
  8.2 0.7 convert_element_type.65
  9.0 0.6 pad_maximum_fusion
  9.7 6.7 %copy.78 = f32[762,16,128]{0,1,2:T(8,128)} copy(f32[762,16,128]{2,1,0:T(8,128)} %param.12) | data formatting | bytes 12484608 | tf_op args[0]
  16.4 6.8 %copy.79 = f32[762,16,128]{0,1,2:T(8,128)} copy(f32[762,16,128]{2,1,0:T(8,128)} %param.13) | data formatting | bytes 12484608 | tf_op args[1]
  23.3 0.6 copy.80
  24.1 11.4 %add_convert_fusion.x_ref = bf16[4,2048,762]{2,1,0:T(8,128)(2,1)} fusion(f32[2048,762]{1,0:T(8,128)} %bitcast.110, f32[4]{0:T(128)S(1)} %copy-done.6, f32[2048,762]{1,0:T(8,128)} %bitcast.109), kind=kLoop, calls=%fused_computation.6 | loop fusion | flops 18726912 | bytes 24969232 | tf_op jit(solution)/shard_map/convert_element_type | solution.py:138
  35.5 39.6 %shard_map.131 = (f32[4,6,2048,128]{3,2,1,0:T(8,128)}, f32[4,6,16,128]{3,2,1,0:T(8,128)S(1)}) custom-call(bf16[4,2048,762]{2,1,0:T(8,128)(2,1)} %add_convert_fusion.x_ref, bf16[762,768]{1,0:T(8,128)(2,1)S(1)} %pad_bitcast_fusion.mix_ref, f32[6,16,128]{2,1,0:T(8,128)S(1)} %broadcast_in_dim.102.a_ref, f32[6,128,128]{2,1,0:T(8,128)S(1)} %broadcast_in_dim.103.b_ref), custom_call_target="tpu_custom_call" | custom-call | flops 9613344768 | bytes 38820864 | tf_op jit(solution)/shard_map/pallas_call | solution.py:63
  75.0 1.6 collective-permute-start.1
  76.7 8.3 %collective-permute-done = f32[4,6,16,128]{3,2,1,0:T(8,128)S(1)} collective-permute-done((f32[4,6,16,128]{3,2,1,0:T(8,128)S(1)}, f32[4,6,16,128]{3,2,1,0:T(8,128)S(1)}, u32[]{:S(2)}, u32[]{:S(2)}) %collective-permute-start) | collective-permute-done | bytes 196640 | tf_op jit(solution)/shard_map/ppermute | solution.py:92
  85.0 1.2 collective-permute-done.1
  86.2 10.7 %collective-permute-done.2 = f32[4,6,16,128]{3,2,1,0:T(8,128)S(1)} collective-permute-done((f32[4,6,16,128]{3,2,1,0:T(8,128)S(1)}, f32[4,6,16,128]{3,2,1,0:T(8,128)S(1)}, u32[]{:S(2)}, u32[]{:S(2)}) %collective-permute-start.2) | collective-permute-done | bytes 196640 | tf_op jit(solution)/shard_map/ppermute | solution.py:92
  97.0 10.6 %collective-permute-done.3 = f32[4,6,16,128]{3,2,1,0:T(8,128)S(1)} collective-permute-done((f32[4,6,16,128]{3,2,1,0:T(8,128)S(1)}, f32[4,6,16,128]{3,2,1,0:T(8,128)S(1)}, u32[]{:S(2)}, u32[]{:S(2)}) %collective-permute-start.3) | collective-permute-done | bytes 196640 | tf_op jit(solution)/shard_map/ppermute | solution.py:92
  107.8 7.3 %collective-permute-done.4 = f32[4,6,16,128]{3,2,1,0:T(8,128)S(1)} collective-permute-done((f32[4,6,16,128]{3,2,1,0:T(8,128)S(1)}, f32[4,6,16,128]{3,2,1,0:T(8,128)S(1)}, u32[]{:S(2)}, u32[]{:S(2)}) %collective-permute-start.4) | collective-permute-done | bytes 196640 | tf_op jit(solution)/shard_map/ppermute | solution.py:92
  115.2 0.3 collective-permute-start.5
  115.6 7.0 %collective-permute-done.5 = f32[4,6,16,128]{3,2,1,0:T(8,128)S(1)} collective-permute-done((f32[4,6,16,128]{3,2,1,0:T(8,128)S(1)}, f32[4,6,16,128]{3,2,1,0:T(8,128)S(1)}, u32[]{:S(2)}, u32[]{:S(2)}) %collective-permute-start.5) | collective-permute-done | bytes 196640 | tf_op jit(solution)/shard_map/ppermute | solution.py:92
  122.9 2.8 fusion.32
  125.9 0.3 stack.8
  126.2 2.5 constant_dynamic-slice_fusion
  128.7 0.8 copy.97
  130.1 6.5 %fusion.46 = f32[1024,2048,1]{1,0,2:T(8,128)} fusion(f32[1024]{0:T(1024)S(1)} %bitcast.118, s32[1024]{0:T(1024)S(1)} %get-tuple-element.37, f32[1024]{0:T(1024)S(1)} %bitcast.119, s32[1024]{0:T(1024)S(1)} %get-tuple-element.38, f32[1024]{0:T(1024)S(1)} %bitcast.120, s32[1024]{0:T(1024)S(1)} %get-tuple-element.36, f32[1024]{0:T(1024)S(1)} %bitcast.117, ...), kind=kLoop, calls=%fused_computation.9.clone.1 | loop fusion | flops 23068672 | bytes 8421376 | tf_op jit(solution)/shard_map/rp,tpn->trn/dot_general | solution.py:210
  136.6 52.5 %all-gather.3.cloned.1.call-done = f32[4,4,6,128,128]{4,3,2,1,0:T(8,128)} async-done(((f32[1,4,6,128,128]{4,3,2,1,0:T(8,128)}), f32[4,4,6,128,128]{4,3,2,1,0:T(8,128)}) %all-gather.3.cloned.1.call-update) | async-done | bytes 6291472 | tf_op jit(solution)/shard_map/all_gather | solution.py:185
  189.1 3.8 %multiply_reduce_fusion.1 = f32[4,6,128,128]{3,2,1,0:T(8,128)S(1)} fusion(f32[4,4,6,128,128]{4,3,2,1,0:T(8,128)} %all-gather.3.cloned.1.call-done, f32[4,6,128]{2,1,0:T(8,128)S(1)} %exponential_select_fusion), kind=kLoop, calls=%fused_computation.24 | loop fusion | flops 2752512 | bytes 7876608 | tf_op jit(solution)/shard_map/reduce_sum | solution.py:194
  192.9 0.8 mul.561
  193.7 0.4 mul.611
  194.1 18.4 %fusion.1 = f32[4,6,2048,128]{3,2,1,0:T(8,128)} fusion(f32[4,6,2048,128]{3,2,1,0:T(8,128)} %get-tuple-element.4, f32[4,6,128,128]{3,2,1,0:T(8,128)S(1)} %multiply_reduce_fusion.1, f32[6,2048,128]{2,1,0:T(8,128)S(1)} %bitcast.108, f32[4,6,16,128]{3,2,1,0:T(8,128)S(1)} %stack.8, f32[6,2048,128]{2,1,0:T(8,128)S(1)} %bitcast.107, ...), kind=kLoop, calls=%fused_computation.2 | loop fusion | flops 37748736 | bytes 64690176 | tf_op jit(solution)/shard_map/mul | solution.py:196
  212.5 24.8 %copy.84 = f32[4,2048,6,128]{1,3,2,0:T(8,128)} copy(f32[4,2048,6,128]{3,1,2,0:T(8,128)} %bitcast.104) | data formatting | bytes 50331648 | tf_op jit(solution)/shard_map/transpose | solution.py:200
  237.3 45.1 %fusion.4 = bf16[4,768,1024]{2,1,0:T(8,128)(2,1)S(1)} fusion(f32[4,2048,768]{1,2,0:T(8,128)} %bitcast.106, f32[1024,2048,1]{1,0,2:T(8,128)} %fusion.46), kind=kOutput, calls=%fused_computation.8 | convolution fusion | flops 38654705664 | bytes 39845888 | tf_op jit(solution)/shard_map/rp,tpn->trn/dot_general | solution.py:210
  282.5 2.3 fusion.27
  284.8 1.9 copy.91
  286.7 1.6 copy.92
  288.3 9.2 %all-to-all-start = ((f32[128,8,4,128]{3,1,2,0:T(8,128)}), f32[128,8,4,128]{3,1,2,0:T(8,128)S(1)}, u32[]{:S(2)}, u32[]{:S(2)}) async-start(f32[128,8,4,128]{3,1,2,0:T(8,128)} %copy.92), calls=%async_computation | async-start | bytes 4194304 | tf_op jit(solution)/shard_map/all_to_all | solution.py:218
  297.6 9.0 %multiply_reduce_fusion = f32[4]{0:T(128)S(1)} fusion(f32[762,16,128]{2,1,0:T(8,128)} %param.13, f32[4]{0:T(128)S(1)} %copy-done.6, f32[762,16,128]{2,1,0:T(8,128)} %param.12), kind=kLoop, calls=%fused_computation.7 | loop fusion | flops 24969212 | bytes 12484640 | tf_op jit(solution)/shard_map/reduce_sum | solution.py:137
  306.7 21.2 %all-to-all-done = f32[128,8,4,128]{3,1,2,0:T(8,128)S(1)} async-done(((f32[128,8,4,128]{3,1,2,0:T(8,128)}), f32[128,8,4,128]{3,1,2,0:T(8,128)S(1)}, u32[]{:S(2)}, u32[]{:S(2)}) %all-to-all-start) | async-done | bytes 2097184 | tf_op jit(solution)/shard_map/all_to_all | solution.py:218
  327.9 0.5 multiply_reduce_fusion.2
  328.5 2.7 copy.94
  331.2 0.7 collective-permute-start.7
  331.8 3.0 collective-permute-done.7
  334.8 0.7 collective-permute-start.8
  335.5 4.5 %collective-permute-done.8 = f32[2,4]{1,0:T(2,128)S(1)} collective-permute-done((f32[2,4]{1,0:T(2,128)S(1)}, f32[2,4]{1,0:T(2,128)S(1)}, u32[]{:S(2)}, u32[]{:S(2)}) %collective-permute-start.8) | collective-permute-done | bytes 64 | tf_op jit(solution)/shard_map/ppermute | solution.py:100
  340.2 3.4 collective-permute-done.9
  343.6 0.2 collective-permute-start.10
  343.8 4.8 %collective-permute-done.10 = f32[2,4]{1,0:T(2,128)S(1)} collective-permute-done((f32[2,4]{1,0:T(2,128)S(1)}, f32[2,4]{1,0:T(2,128)S(1)}, u32[]{:S(2)}, u32[]{:S(2)}) %collective-permute-start.10) | collective-permute-done | bytes 64 | tf_op jit(solution)/shard_map/ppermute | solution.py:100
  348.6 0.4 collective-permute-start.11
  349.0 3.2 collective-permute-done.11
  352.2 0.4 collective-permute-start.12
  352.6 4.7 %collective-permute-done.12 = f32[2,4]{1,0:T(2,128)S(1)} collective-permute-done((f32[2,4]{1,0:T(2,128)S(1)}, f32[2,4]{1,0:T(2,128)S(1)}, u32[]{:S(2)}, u32[]{:S(2)}) %collective-permute-start.12) | collective-permute-done | bytes 64 | tf_op jit(solution)/shard_map/ppermute | solution.py:100
  357.3 0.5 multiply_bitcast_fusion
  (70 shorter events, 2.4 us)
Async XLA Ops:
  7.2 119.1 %all-gather.5.cloned.1.call-start = ((), (), s32[]{:S(2)}) async-start(), calls=%async_computation.2 | async-start | bytes 2641920 | tf_op jit(solution)/shard_map/all_gather | solution.py:133
  9.7 179.4 %all-gather.3.cloned.1.call-start = ((), (), s32[]{:S(2)}) async-start(), calls=%async_computation.1 | async-start | bytes 7864320 | tf_op jit(solution)/shard_map/all_gather | solution.py:185
  16.4 6.8 %copy-start = (bf16[762,762]{1,0:T(8,128)(2,1)S(1)}, bf16[762,762]{1,0:T(8,128)(2,1)}, u32[]{:S(2)}) copy-start(bf16[762,762]{1,0:T(8,128)(2,1)} %param.15) | copy-start | bytes 3483868
  16.4 7.5 %copy-start.5 = (f32[762]{0:T(1024)S(1)}, f32[762]{0:T(1024)}, u32[]{:S(2)}) copy-start(f32[762]{0:T(1024)} %param.17) | copy-start | bytes 9148
  16.4 7.5 %copy-start.4 = (f32[762]{0:T(1024)S(1)}, f32[762]{0:T(1024)}, u32[]{:S(2)}) copy-start(f32[762]{0:T(1024)} %param.16) | copy-start | bytes 9148
  16.4 7.7 %copy-start.6 = (f32[4]{0:T(128)S(1)}, f32[4]{0:T(128)}, u32[]{:S(2)}) copy-start(f32[4]{0:T(128)} %param.14) | copy-start | bytes 52
  75.0 9.9 %collective-permute-start = (f32[4,6,16,128]{3,2,1,0:T(8,128)S(1)}, f32[4,6,16,128]{3,2,1,0:T(8,128)S(1)}, u32[]{:S(2)}, u32[]{:S(2)}) collective-permute-start(f32[4,6,16,128]{3,2,1,0:T(8,128)S(1)} %get-tuple-element.5), channel_id=1, source_target_pairs={{0,1},{1,2},{2,3},{3,4},{4,5},{5,6},{6,7},{7,8},{8,9},{9,10},{10,1... | collective-permute-start | bytes 589832 | tf_op jit(solution)/shard_map/ppermute | solution.py:92
  75.0 11.1 %collective-permute-start.1 = (f32[4,6,16,128]{3,2,1,0:T(8,128)S(1)}, f32[4,6,16,128]{3,2,1,0:T(8,128)S(1)}, u32[]{:S(2)}, u32[]{:S(2)}) collective-permute-start(f32[4,6,16,128]{3,2,1,0:T(8,128)S(1)} %get-tuple-element.5), channel_id=1, source_target_pairs={{0,2},{1,3},{2,4},{3,5},{4,6},{5,7},{6,8},{7,9},{8,10},{9,11},{10,... | collective-permute-start | bytes 589832 | tf_op jit(solution)/shard_map/ppermute | solution.py:92
  86.2 10.8 %collective-permute-start.2 = (f32[4,6,16,128]{3,2,1,0:T(8,128)S(1)}, f32[4,6,16,128]{3,2,1,0:T(8,128)S(1)}, u32[]{:S(2)}, u32[]{:S(2)}) collective-permute-start(f32[4,6,16,128]{3,2,1,0:T(8,128)S(1)} %multiply_add_fusion.3), channel_id=1, source_target_pairs={{0,2},{1,3},{2,4},{3,5},{4,6},{5,7},{6,8},{7,9},{8,10},{9,11},{10,... | collective-permute-start | bytes 589832 | tf_op jit(solution)/shard_map/ppermute | solution.py:92
  97.0 10.7 %collective-permute-start.3 = (f32[4,6,16,128]{3,2,1,0:T(8,128)S(1)}, f32[4,6,16,128]{3,2,1,0:T(8,128)S(1)}, u32[]{:S(2)}, u32[]{:S(2)}) collective-permute-start(f32[4,6,16,128]{3,2,1,0:T(8,128)S(1)} %multiply_add_fusion.2), channel_id=1, source_target_pairs={{0,4},{1,5},{2,6},{3,7},{4,8},{5,9},{6,10},{7,11},{8,12},{9,13},{1... | collective-permute-start | bytes 589832 | tf_op jit(solution)/shard_map/ppermute | solution.py:92
  107.7 7.4 %collective-permute-start.4 = (f32[4,6,16,128]{3,2,1,0:T(8,128)S(1)}, f32[4,6,16,128]{3,2,1,0:T(8,128)S(1)}, u32[]{:S(2)}, u32[]{:S(2)}) collective-permute-start(f32[4,6,16,128]{3,2,1,0:T(8,128)S(1)} %multiply_add_fusion.1), channel_id=1, source_target_pairs={{0,8},{1,9},{2,10},{3,11},{4,12},{5,13},{6,14},{7,15},{8,16},{9,17... | collective-permute-start | bytes 589832 | tf_op jit(solution)/shard_map/ppermute | solution.py:92
  115.2 7.4 %collective-permute-start.5 = (f32[4,6,16,128]{3,2,1,0:T(8,128)S(1)}, f32[4,6,16,128]{3,2,1,0:T(8,128)S(1)}, u32[]{:S(2)}, u32[]{:S(2)}) collective-permute-start(f32[4,6,16,128]{3,2,1,0:T(8,128)S(1)} %multiply_add_fusion), channel_id=1, source_target_pairs={{0,16},{1,17},{2,18},{3,19},{4,20},{5,21},{6,22},{7,23},{8,24},{9,... | collective-permute-start | bytes 589832 | tf_op jit(solution)/shard_map/ppermute | solution.py:92
  237.3 45.2 %copy-start.3 = (bf16[128,762]{1,0:T(8,128)(2,1)S(1)}, bf16[128,762]{1,0:T(8,128)(2,1)}, u32[]{:S(2)}) copy-start(bf16[128,762]{1,0:T(8,128)(2,1)} %param.18) | copy-start | bytes 585220
  284.8 12.7 %copy-start.7 = (s32[1,128]{1,0:T(1,128)S(1)}, s32[1,128]{1,0:T(1,128)}, u32[]{:S(2)}) copy-start(s32[1,128]{1,0:T(1,128)} %param.23) | copy-start | bytes 1540
  288.3 39.5 %all-to-all-start = ((f32[128,8,4,128]{3,1,2,0:T(8,128)}), f32[128,8,4,128]{3,1,2,0:T(8,128)S(1)}, u32[]{:S(2)}, u32[]{:S(2)}) async-start(f32[128,8,4,128]{3,1,2,0:T(8,128)} %copy.92), calls=%async_computation | async-start | bytes 4194304 | tf_op jit(solution)/shard_map/all_to_all | solution.py:218
  297.5 30.4 %copy-start.1 = (f32[1024,128]{1,0:T(8,128)S(1)}, f32[1024,128]{1,0:T(8,128)}, u32[]{:S(2)}) copy-start(f32[1024,128]{1,0:T(8,128)} %param.20) | copy-start | bytes 1572868
  297.5 30.4 %copy-start.2 = (f32[1024,128]{1,0:T(8,128)S(1)}, f32[1024,128]{1,0:T(8,128)}, u32[]{:S(2)}) copy-start(f32[1024,128]{1,0:T(8,128)} %param.19) | copy-start | bytes 1572868
  328.4 2.8 collective-permute-start.6
  331.2 3.7 %collective-permute-start.7 = (f32[2,4]{1,0:T(2,128)S(1)}, f32[2,4]{1,0:T(2,128)S(1)}, u32[]{:S(2)}, u32[]{:S(2)}) collective-permute-start(f32[2,4]{1,0:T(2,128)S(1)} %fusion.37), channel_id=1, source_target_pairs={{0,2},{1,3},{2,0},{3,1},{4,6},{5,7},{6,4},{7,5},{8,10},{9,11},{10,... | collective-permute-start | bytes 104 | tf_op jit(solution)/shard_map/ppermute | solution.py:100
  334.8 5.2 %collective-permute-start.8 = (f32[2,4]{1,0:T(2,128)S(1)}, f32[2,4]{1,0:T(2,128)S(1)}, u32[]{:S(2)}, u32[]{:S(2)}) collective-permute-start(f32[2,4]{1,0:T(2,128)S(1)} %fusion.42), channel_id=1, source_target_pairs={{0,4},{1,5},{2,6},{3,7},{4,0},{5,1},{6,2},{7,3},{8,12},{9,13},{10,... | collective-permute-start | bytes 104 | tf_op jit(solution)/shard_map/ppermute | solution.py:100
  340.0 3.6 collective-permute-start.9
  343.6 5.1 %collective-permute-start.10 = (f32[2,4]{1,0:T(2,128)S(1)}, f32[2,4]{1,0:T(2,128)S(1)}, u32[]{:S(2)}, u32[]{:S(2)}) collective-permute-start(f32[2,4]{1,0:T(2,128)S(1)} %add.382), channel_id=1, source_target_pairs={{0,16},{1,17},{2,18},{3,19},{4,20},{5,21},{6,22},{7,23},{8,24},{9,... | collective-permute-start | bytes 104 | tf_op jit(solution)/shard_map/ppermute | solution.py:100
  348.6 3.6 collective-permute-start.11
  352.2 5.1 %collective-permute-start.12 = (f32[2,4]{1,0:T(2,128)S(1)}, f32[2,4]{1,0:T(2,128)S(1)}, u32[]{:S(2)}, u32[]{:S(2)}) collective-permute-start(f32[2,4]{1,0:T(2,128)S(1)} %add.384), channel_id=1, source_target_pairs={{0,64},{32,96},{64,0},{96,32},{1,65},{33,97},{65,1},{97,33},{2,66}... | collective-permute-start | bytes 104 | tf_op jit(solution)/shard_map/ppermute | solution.py:100
Sparse Core Ops, SparseCore 0:
  11.1 68.0 all-gather.4
  125.8 63.2 all-gather.2
